TPU v7x, 256 devices: a whole 4x4x8 slice. The times are simulated.
256 devices in a mesh: row: 8 (over z), col: 32 (over y, x, core).
Axes of the slice: x: 4, y: 4, z: 8, core: 2. Of those that a mesh axis runs over, the one named last changes fastest.
Arguments:
- tokens: bfloat16 [512, 8192], P('col', 'row'), may hold values from -6 to 6
- cotangent: bfloat16 [512, 8192], P('col', 'row'), may hold values from -6 to 6
- w_gate: bfloat16 [8192, 16384], P('row', 'col'), may hold values from -0.09375 to 0.09375
- w_up: bfloat16 [8192, 16384], P('row', 'col'), may hold values from -0.09375 to 0.09375
- w_down: bfloat16 [16384, 8192], P('col', 'row'), may hold values from -0.0625 to 0.0625
- order_gate: int32 [2048], replicated, may hold values from 0 to 2047, each once
- order_up: int32 [2048], replicated, may hold values from 0 to 2047, each once
- order_down: int32 [2048], replicated, may hold values from 0 to 2047, each once
Outputs:
- output: bfloat16 [512, 8192], P('col', 'row')
- input_grad: bfloat16 [512, 8192], P('col', 'row')
- gate_weight_grad: float32 [8192, 16384], P('row', 'col')
- up_weight_grad: float32 [8192, 16384], P('row', 'col')
- down_weight_grad: float32 [16384, 8192], P('col', 'row')
Inputs may be any that keep to these rules, and one draw needn't show every extreme that they name: `order_gate`: each of the 2048 block numbers appears exactly once. `order_up`: each of the 2048 block numbers appears exactly once. `order_down`: each of the 2048 block numbers appears exactly once.
All inputs are finite; a program needn't handle non-finite values.
Results may differ from a plain program's by a relative error of at most 0.0049.
Values may be sent and summed in bfloat16 or wider, within the bound.
No kernel may reach another device: no remote copies, remote signals or barrier semaphores. Data moves between devices by JAX's collectives and lax.ppermute only.
A program may use at most 64 MiB of HBM per device.

v0:
```python
import jax
import jax.numpy as jnp
from jax import lax
from jax.sharding import PartitionSpec as P

BLOCK = 256


def kept_table(order, row_first, col_first, row_count, col_count, stride):
    kept_count = order.shape[0] // 2
    row_ids = row_first + jnp.arange(row_count, dtype=jnp.int32)
    col_ids = col_first + jnp.arange(col_count, dtype=jnp.int32)
    block_ids = row_ids[:, None] * stride + col_ids[None, :]
    return jnp.any(block_ids[:, :, None] == order[:kept_count][None, None, :], axis=2)


def expand_mask(kept_mask):
    row_count, col_count = kept_mask.shape
    spread = jnp.broadcast_to(kept_mask[:, None, :, None], (row_count, BLOCK, col_count, BLOCK))
    return spread.reshape(row_count * BLOCK, col_count * BLOCK)


def dense_apply(left_operand, right_operand, kept_mask, product_kind):
    full_mask = expand_mask(kept_mask)
    if product_kind == "forward":
        masked = right_operand * full_mask.astype(right_operand.dtype)
        return jnp.dot(left_operand, masked, preferred_element_type=jnp.float32)
    if product_kind == "transposed":
        masked = right_operand * full_mask.astype(right_operand.dtype)
        return lax.dot_general(
            left_operand, masked, (((1,), (1,)), ((), ())), preferred_element_type=jnp.float32
        )
    product = lax.dot_general(
        left_operand, right_operand, (((0,), (0,)), ((), ())), preferred_element_type=jnp.float32
    )
    return product * full_mask.astype(jnp.float32)


def apply_blocks(left_operand, right_operand, kept_mask, product_kind):
    return dense_apply(left_operand, right_operand, kept_mask, product_kind)


def on_device(tokens, cotangent, w_gate, w_up, w_down, order_gate, order_up, order_down):
    rows_here = w_gate.shape[0] // BLOCK
    cols_here = w_gate.shape[1] // BLOCK
    row_start = lax.axis_index("row") * rows_here
    col_start = lax.axis_index("col") * cols_here
    width_blocks = rows_here * lax.axis_size("row")
    hidden_blocks = cols_here * lax.axis_size("col")
    keep_gate = kept_table(order_gate, row_start, col_start, rows_here, cols_here, hidden_blocks)
    keep_up = kept_table(order_up, row_start, col_start, rows_here, cols_here, hidden_blocks)
    keep_down = kept_table(order_down, col_start, row_start, cols_here, rows_here, width_blocks)
    tokens_all = lax.all_gather(tokens, "col", axis=0, tiled=True)
    gate_term = apply_blocks(tokens_all, w_gate, keep_gate, "forward")
    up_term = apply_blocks(tokens_all, w_up, keep_up, "forward")
    gate, up = (
        lax.psum_scatter(gate_term, "row", scatter_dimension=0, tiled=True),
        lax.psum_scatter(up_term, "row", scatter_dimension=0, tiled=True),
    )
    sigmoid_gate = jax.nn.sigmoid(gate)
    activation = gate * sigmoid_gate
    hidden = (activation * up).astype(jnp.bfloat16)
    hidden_all = lax.all_gather(hidden, "row", axis=0, tiled=True)
    output_term = apply_blocks(hidden_all, w_down, keep_down, "forward")
    output = lax.psum_scatter(output_term, "col", scatter_dimension=0, tiled=True).astype(
        jnp.bfloat16
    )
    cotangent_all = lax.all_gather(cotangent, "col", axis=0, tiled=True)
    hidden_term = apply_blocks(cotangent_all, w_down, keep_down, "transposed")
    hidden_grad = lax.psum_scatter(hidden_term, "row", scatter_dimension=0, tiled=True)
    gate_grad = (hidden_grad * up * sigmoid_gate * (1.0 + gate * (1.0 - sigmoid_gate))).astype(
        jnp.bfloat16
    )
    up_grad = (hidden_grad * activation).astype(jnp.bfloat16)
    gate_grad_all, up_grad_all = (
        lax.all_gather(gate_grad, "row", axis=0, tiled=True),
        lax.all_gather(up_grad, "row", axis=0, tiled=True),
    )
    down_weight_grad = apply_blocks(hidden_all, cotangent_all, keep_down, "weights")
    gate_weight_grad = apply_blocks(tokens_all, gate_grad_all, keep_gate, "weights")
    up_weight_grad = apply_blocks(tokens_all, up_grad_all, keep_up, "weights")
    through_gate = apply_blocks(gate_grad_all, w_gate, keep_gate, "transposed")
    through_up = apply_blocks(up_grad_all, w_up, keep_up, "transposed")
    gate_share = lax.psum_scatter(through_gate, "col", scatter_dimension=0, tiled=True)
    up_share = lax.psum_scatter(through_up, "col", scatter_dimension=0, tiled=True)
    input_grad = gate_share + up_share
    return (
        output,
        input_grad.astype(jnp.bfloat16),
        gate_weight_grad,
        up_weight_grad,
        down_weight_grad,
    )


def solution(mesh):
    placed = (
        P("col", "row"),
        P("col", "row"),
        P("row", "col"),
        P("row", "col"),
        P("col", "row"),
        P(),
        P(),
        P(),
    )
    return jax.shard_map(
        on_device,
        mesh=mesh,
        in_specs=placed,
        out_specs=(
            P("col", "row"),
            P("col", "row"),
            P("row", "col"),
            P("row", "col"),
            P("col", "row"),
        ),
        check_vma=False,
    )
```

profile of v0, /device:TPU:2, one launch (start us, length us, event | category | flops | bytes accessed | tf_op | source)
XLA Modules:
  0.0 445.8 jit_solution(2200922386354329133)
XLA Ops:
  10.3 50.4 %all-gather.5.cloned.1.call-done = bf16[512,1024]{1,0:T(8,128)(2,1)} async-done(((bf16[16,1024]{1,0:T(8,128)(2,1)}), bf16[512,1024]{1,0:T(8,128)(2,1)}) %all-gather.5.cloned.1.call-update) | async-done | bytes 1048592 | tf_op jit(solution)/shard_map/all_gather | solution.py:68
  60.8 2.3 convolution_bitcast_fusion
  65.9 44.4 %all-gather.3.cloned.1.call-done = bf16[512,1024]{1,0:T(8,128)(2,1)} async-done(((bf16[16,1024]{1,0:T(8,128)(2,1)}), bf16[512,1024]{1,0:T(8,128)(2,1)}) %all-gather.3.cloned.1.call-update) | async-done | bytes 1048592 | tf_op jit(solution)/shard_map/all_gather | solution.py:53
  110.3 2.0 convolution_bitcast_fusion.2
  114.3 1.7 copy.34
  116.0 2.9 convolution_bitcast_fusion.1
  118.9 2.5 copy.44
  121.6 30.7 %reduce-scatter.20.cloned.1.call-done = f32[64,512]{1,0:T(8,128)} async-done(((f32[512,512]{1,0:T(8,128)}), f32[64,512]{1,0:T(8,128)}) %reduce-scatter.20.cloned.1.call-update) | async-done | bytes 131088 | tf_op jit(solution)/shard_map/reduce_scatter | solution.py:70
  152.3 40.6 %reduce-scatter.16.cloned.1.call-done = f32[64,512]{1,0:T(8,128)} async-done(((f32[512,512]{1,0:T(8,128)}), f32[64,512]{1,0:T(8,128)}) %reduce-scatter.16.cloned.1.call-update) | async-done | bytes 131088 | tf_op jit(solution)/shard_map/reduce_scatter | solution.py:57
  192.9 40.0 %reduce-scatter.18.cloned.1.call-done = f32[64,512]{1,0:T(8,128)} async-done(((f32[512,512]{1,0:T(8,128)}), f32[64,512]{1,0:T(8,128)}) %reduce-scatter.18.cloned.1.call-update) | async-done | bytes 131088 | tf_op jit(solution)/shard_map/reduce_scatter | solution.py:58
  234.1 25.5 %all_gather.16 = bf16[512,512]{1,0:T(8,128)(2,1)S(1)} all-gather(bf16[64,512]{1,0:T(8,128)(2,1)S(1)} %get-tuple-element.29), channel_id=1, replica_groups=mesh['row'=8,'col'=32] {'row'}, dimensions={0}, use_global_device_ids=true | all-gather | bytes 589824 | tf_op jit(solution)/shard_map/all_gather | solution.py:63
  259.6 3.3 fusion.1
  262.9 25.5 %all_gather.18 = bf16[512,512]{1,0:T(8,128)(2,1)S(1)} all-gather(bf16[64,512]{1,0:T(8,128)(2,1)S(1)} %get-tuple-element.28), channel_id=1, replica_groups=mesh['row'=8,'col'=32] {'row'}, dimensions={0}, use_global_device_ids=true | all-gather | bytes 589824 | tf_op jit(solution)/shard_map/all_gather | solution.py:76
  288.4 25.2 %all_gather.19 = bf16[512,512]{1,0:T(8,128)(2,1)S(1)} all-gather(bf16[64,512]{1,0:T(8,128)(2,1)S(1)} %get-tuple-element.27), channel_id=1, replica_groups=mesh['row'=8,'col'=32] {'row'}, dimensions={0}, use_global_device_ids=true | all-gather | bytes 589824 | tf_op jit(solution)/shard_map/all_gather | solution.py:77
  313.7 2.0 fusion.9
  315.7 2.1 convolution_add_fusion
  319.1 2.0 bitcast_select_fusion.1
  321.2 3.0 copy.40
  324.2 2.1 bitcast_select_fusion
  326.2 3.0 copy.41
  329.2 2.0 convolution_select_fusion
  331.3 16.4 %reduce-scatter.12.cloned.1.call-done = f32[16,1024]{1,0:T(8,128)} async-done(((f32[512,1024]{1,0:T(8,128)}), f32[16,1024]{1,0:T(8,128)}) %reduce-scatter.12.cloned.1.call-update) | async-done | bytes 65552 | tf_op jit(solution)/shard_map/reduce_scatter | solution.py:65
  349.1 88.4 %reduce-scatter.14.cloned.1.call-done = f32[16,1024]{1,0:T(8,128)} async-done(((f32[512,1024]{1,0:T(8,128)}), f32[16,1024]{1,0:T(8,128)}) %reduce-scatter.14.cloned.1.call-update) | async-done | bytes 65552 | tf_op jit(solution)/shard_map/reduce_scatter | solution.py:84
  437.5 1.5 convert_element_type.28
  (60 shorter events, 12.0 us)
Async XLA Ops:
  7.2 53.6 %all-gather.5.cloned.1.call-start = ((), (), s32[]{:S(2)}) async-start(), calls=%async_computation.7 | async-start | bytes 1081344 | tf_op jit(solution)/shard_map/all_gather | solution.py:68
  7.9 102.4 %all-gather.3.cloned.1.call-start = ((), (), s32[]{:S(2)}) async-start(), calls=%async_computation.5 | async-start | bytes 1081344 | tf_op jit(solution)/shard_map/all_gather | solution.py:53
  8.6 143.6 %reduce-scatter.20.cloned.1.call-start = ((), (), s32[]{:S(2)}) async-start(), calls=%async_computation.11 | async-start | bytes 1179648 | tf_op jit(solution)/shard_map/reduce_scatter | solution.py:70
  10.3 249.3 %copy-start.5 = (pred[64,8,4,256]{3,1,2,0:T(8,128)(4,1)}, pred[64,8,4,256]{3,1,2,0:T(8,128)(4,1)S(1)}, u32[]{:S(2)}) copy-start(pred[64,8,4,256]{3,1,2,0:T(8,128)(4,1)S(1)} %copy.50) | copy-start | bytes 1572868
  63.0 1.5 slice-start
  63.1 1.5 slice-start.1
  63.1 2.3 copy-start.9
  64.4 128.5 %reduce-scatter.16.cloned.1.call-start = ((), (), s32[]{:S(2)}) async-start(), calls=%async_computation.9 | async-start | bytes 1179648 | tf_op jit(solution)/shard_map/reduce_scatter | solution.py:57
  65.4 46.9 %copy-start.7 = (pred[64,8,4,256]{3,1,2,0:T(8,128)(4,1)}, pred[64,8,4,256]{3,1,2,0:T(8,128)(4,1)S(1)}, u32[]{:S(2)}) copy-start(pred[64,8,4,256]{3,1,2,0:T(8,128)(4,1)S(1)} %copy.48) | copy-start | bytes 1572868
  113.6 119.3 %reduce-scatter.18.cloned.1.call-start = ((), (), s32[]{:S(2)}) async-start(), calls=%async_computation.10 | async-start | bytes 1179648 | tf_op jit(solution)/shard_map/reduce_scatter | solution.py:58
  114.3 4.6 %copy-start = (pred[64,8,4,256]{3,1,2,0:T(8,128)(4,1)}, pred[64,8,4,256]{3,1,2,0:T(8,128)(4,1)S(1)}, u32[]{:S(2)}) copy-start(pred[64,8,4,256]{3,1,2,0:T(8,128)(4,1)S(1)} %copy.49) | copy-start | bytes 1572868
  121.5 226.2 %reduce-scatter.12.cloned.1.call-start = ((), (), s32[]{:S(2)}) async-start(), calls=%async_computation.6 | async-start | bytes 2162688 | tf_op jit(solution)/shard_map/reduce_scatter | solution.py:65
  262.9 174.6 %reduce-scatter.14.cloned.1.call-start = ((), (), s32[]{:S(2)}) async-start(), calls=%async_computation.8 | async-start | bytes 2162688 | tf_op jit(solution)/shard_map/reduce_scatter | solution.py:84
  313.7 2.0 copy-start.3
  313.7 2.0 copy-start.1
  317.7 1.0 copy-start.8
  317.7 1.4 copy-start.11
  321.2 3.0 copy-start.2
  321.2 3.0 copy-start.4
  326.2 3.0 copy-start.6
  326.2 3.0 copy-start.10
Sparse Core Ops, SparseCore 0:
  10.5 50.1 all-gather.4
  63.3 46.9 all-gather.2
  113.4 38.7 reduce-scatter.19
  155.2 37.6 reduce-scatter.15
  195.3 37.6 reduce-scatter.17
  263.0 84.6 reduce-scatter.11
  351.5 85.9 reduce-scatter.13
where the time goes:
time: 446 us
  waiting for transfers between devices  312 us (70%)
  blocking collectives  76.2 us (17%)
  matrix products  20.7 us (5%)
  local copies, waits for them, and re-layouts  17.3 us (4%)
  between operations  14.3 us (3%)
  other arithmetic  4.62 us (1%)
    reduce_scatter x1, waiting for transfers between devices, on_device(): lax.psum_scatter(through_gate, 'col', scatter_dimension=0, tiled=True)  88.4 us
    all_gather x1, waiting for transfers between devices, on_device(): cotangent_all = lax.all_gather(cotangent, 'col', axis=0, tiled=True)  50.4 us
    all_gather x1, waiting for transfers between devices, on_device(): tokens_all = lax.all_gather(tokens, 'col', axis=0, tiled=True)  44.4 us
    reduce_scatter x1, waiting for transfers between devices, on_device(): lax.psum_scatter(gate_term, 'row', scatter_dimension=0, tiled=True)  40.6 us
    reduce_scatter x1, waiting for transfers between devices, on_device(): lax.psum_scatter(up_term, 'row', scatter_dimension=0, tiled=True)  40 us
    reduce_scatter x1, waiting for transfers between devices, on_device(): lax.psum_scatter(hidden_term, 'row', scatter_dimension=0, tiled=True)  30.7 us
    all_gather x1, blocking collectives, on_device(): hidden_all = lax.all_gather(hidden, 'row', axis=0, tiled=True)  25.5 us
    all_gather x1, blocking collectives, on_device(): lax.all_gather(gate_grad, 'row', axis=0, tiled=True)  25.5 us
  transfers between devices with their start and end apart: 7, of which 7 were waited for; matrix products, arithmetic and copies ran while one was open for 8% of the time, Pallas kernels for 0%

commit v1 on v0

--- a/solution.py
+++ b/solution.py
@@ -50,7 +50,9 @@
     keep_gate = kept_table(order_gate, row_start, col_start, rows_here, cols_here, hidden_blocks)
     keep_up = kept_table(order_up, row_start, col_start, rows_here, cols_here, hidden_blocks)
     keep_down = kept_table(order_down, col_start, row_start, cols_here, rows_here, width_blocks)
-    tokens_all = lax.all_gather(tokens, "col", axis=0, tiled=True)
+    tokens_all = jnp.concatenate(
+        lax.all_to_all(jnp.stack([tokens] * lax.axis_size("col")), "col", 0, 0), axis=0
+    )
     gate_term = apply_blocks(tokens_all, w_gate, keep_gate, "forward")
     up_term = apply_blocks(tokens_all, w_up, keep_up, "forward")
     gate, up = (

time: 446 us -> 372 us (0.83)
  waiting for transfers between devices: 312 us -> 223 us
  starting transfers between devices: 0.28 us -> 8.06 us
    all_gather x1 -> x0, waiting for transfers between devices: 44.4 us -> none  [on_device(): tokens_all = lax.all_gather(tokens, 'col', axis=0, tiled=True)]
    all_gather x1, waiting for transfers between devices: 50.4 us -> 16.8 us  [on_device(): cotangent_all = lax.all_gather(cotangent, 'col', axis=0, tiled=True)]
    reduce_scatter x1, waiting for transfers between devices: 40.6 us -> 7.82 us  [on_device(): lax.psum_scatter(gate_term, 'row', scatter_dimension=0, tiled=True)]
    all_to_all x0 -> x1, waiting for transfers between devices: none -> 14.7 us  [on_device(): lax.all_to_all(jnp.stack([tokens] * lax.axis_size('col')), 'col', 0, 0)]
    reduce_scatter x1, waiting for transfers between devices: 30.7 us -> 40.6 us  [on_device(): lax.psum_scatter(hidden_term, 'row', scatter_dimension=0, tiled=True)]
    all_to_all x0 -> x1, starting transfers between devices: none -> 7.8 us  [on_device(): lax.all_to_all(jnp.stack([tokens] * lax.axis_size('col')), 'col', 0, 0)]
    unnamed x34 -> x32, local copies, waits for them, and re-layouts: 15.5 us -> 16.4 us
  transfers between devices with their start and end apart: 7 -> 7, of which waited for: 7 -> 7; matrix products, arithmetic and copies ran while one was open for 8% -> 11% of each run, Pallas kernels for 0% -> 0%
where the time goes in v1:
time: 372 us; the launch traced here: 371 us
  waiting for transfers between devices  223 us (60%)
  blocking collectives  76.2 us (20%)
  matrix products  24.1 us (6%)
  local copies, waits for them, and re-layouts  19.3 us (5%)
  between operations  15.6 us (4%)
  starting transfers between devices  8.06 us (2%)
  other arithmetic  4.62 us (1%)
    reduce_scatter x1, waiting for transfers between devices, on_device(): lax.psum_scatter(through_gate, 'col', scatter_dimension=0, tiled=True)  88.4 us
    reduce_scatter x1, waiting for transfers between devices, on_device(): lax.psum_scatter(hidden_term, 'row', scatter_dimension=0, tiled=True)  40.6 us
    reduce_scatter x1, waiting for transfers between devices, on_device(): lax.psum_scatter(up_term, 'row', scatter_dimension=0, tiled=True)  39.9 us
    all_gather x1, blocking collectives, on_device(): lax.all_gather(gate_grad, 'row', axis=0, tiled=True)  25.7 us
    all_gather x1, blocking collectives, on_device(): hidden_all = lax.all_gather(hidden, 'row', axis=0, tiled=True)  25.4 us
    all_gather x1, blocking collectives, on_device(): lax.all_gather(up_grad, 'row', axis=0, tiled=True)  25.2 us
    all_gather x1, waiting for transfers between devices, on_device(): cotangent_all = lax.all_gather(cotangent, 'col', axis=0, tiled=True)  16.8 us
    unnamed x32, local copies, waits for them, and re-layouts  16.4 us
  transfers between devices with their start and end apart: 7, of which 7 were waited for; matrix products, arithmetic and copies ran while one was open for 11% of the time, Pallas kernels for 0%

profile of v1, /device:TPU:2, one launch (start us, length us, event | category | flops | bytes accessed | tf_op | source)
XLA Modules:
  0.0 371.4 jit_solution(10322259020676261030)
XLA Ops:
  10.6 7.8 %all-to-all-start = ((bf16[32,16,1024]{2,1,0:T(8,128)(2,1)}), bf16[32,16,1024]{2,1,0:T(8,128)(2,1)}, u32[]{:S(2)}, u32[]{:S(2)}) async-start(bf16[32,16,1024]{2,1,0:T(8,128)(2,1)} %stack.2), calls=%async_computation | async-start | bytes 2097152 | tf_op jit(solution)/shard_map/all_to_all | solution.py:54
  20.0 14.7 %all-to-all-done = bf16[32,16,1024]{2,1,0:T(8,128)(2,1)} async-done(((bf16[32,16,1024]{2,1,0:T(8,128)(2,1)}), bf16[32,16,1024]{2,1,0:T(8,128)(2,1)}, u32[]{:S(2)}, u32[]{:S(2)}) %all-to-all-start) | async-done | bytes 1048608 | tf_op jit(solution)/shard_map/all_to_all | solution.py:54
  34.7 2.0 convolution_bitcast_fusion.2
  40.3 2.9 convolution_bitcast_fusion.1
  43.3 2.6 copy.44
  46.9 16.8 %all-gather.2.cloned.1.call-done = bf16[512,1024]{1,0:T(8,128)(2,1)} async-done(((bf16[16,1024]{1,0:T(8,128)(2,1)}), bf16[512,1024]{1,0:T(8,128)(2,1)}) %all-gather.2.cloned.1.call-update) | async-done | bytes 1048592 | tf_op jit(solution)/shard_map/all_gather | solution.py:70
  63.7 3.3 convolution_bitcast_fusion
  66.9 2.5 copy.46
  69.5 7.8 %reduce-scatter.16.cloned.1.call-done = f32[64,512]{1,0:T(8,128)} async-done(((f32[512,512]{1,0:T(8,128)}), f32[64,512]{1,0:T(8,128)}) %reduce-scatter.16.cloned.1.call-update) | async-done | bytes 131088 | tf_op jit(solution)/shard_map/reduce_scatter | solution.py:59
  77.4 39.9 %reduce-scatter.18.cloned.1.call-done = f32[64,512]{1,0:T(8,128)} async-done(((f32[512,512]{1,0:T(8,128)}), f32[64,512]{1,0:T(8,128)}) %reduce-scatter.18.cloned.1.call-update) | async-done | bytes 131088 | tf_op jit(solution)/shard_map/reduce_scatter | solution.py:60
  117.3 40.6 %reduce-scatter.20.cloned.1.call-done = f32[64,512]{1,0:T(8,128)} async-done(((f32[512,512]{1,0:T(8,128)}), f32[64,512]{1,0:T(8,128)}) %reduce-scatter.20.cloned.1.call-update) | async-done | bytes 131088 | tf_op jit(solution)/shard_map/reduce_scatter | solution.py:72
  159.0 25.4 %all_gather.12 = bf16[512,512]{1,0:T(8,128)(2,1)S(1)} all-gather(bf16[64,512]{1,0:T(8,128)(2,1)S(1)} %get-tuple-element.29), channel_id=1, replica_groups=mesh['row'=8,'col'=32] {'row'}, dimensions={0}, use_global_device_ids=true | all-gather | bytes 589824 | tf_op jit(solution)/shard_map/all_gather | solution.py:65
  184.3 3.3 fusion.1
  187.7 25.7 %all_gather.14 = bf16[512,512]{1,0:T(8,128)(2,1)S(1)} all-gather(bf16[64,512]{1,0:T(8,128)(2,1)S(1)} %get-tuple-element.28), channel_id=1, replica_groups=mesh['row'=8,'col'=32] {'row'}, dimensions={0}, use_global_device_ids=true | all-gather | bytes 589824 | tf_op jit(solution)/shard_map/all_gather | solution.py:78
  213.4 25.2 %all_gather.15 = bf16[512,512]{1,0:T(8,128)(2,1)S(1)} all-gather(bf16[64,512]{1,0:T(8,128)(2,1)S(1)} %get-tuple-element.27), channel_id=1, replica_groups=mesh['row'=8,'col'=32] {'row'}, dimensions={0}, use_global_device_ids=true | all-gather | bytes 589824 | tf_op jit(solution)/shard_map/all_gather | solution.py:79
  238.6 2.0 fusion.9
  240.6 2.1 convolution_add_fusion
  243.7 3.3 bitcast_select_fusion.1
  247.0 3.0 copy.40
  250.0 3.3 bitcast_select_fusion
  253.2 3.0 copy.41
  256.2 2.0 convolution_select_fusion
  258.3 14.5 %reduce-scatter.12.cloned.1.call-done = f32[16,1024]{1,0:T(8,128)} async-done(((f32[512,1024]{1,0:T(8,128)}), f32[16,1024]{1,0:T(8,128)}) %reduce-scatter.12.cloned.1.call-update) | async-done | bytes 65552 | tf_op jit(solution)/shard_map/reduce_scatter | solution.py:67
  274.2 88.4 %reduce-scatter.14.cloned.1.call-done = f32[16,1024]{1,0:T(8,128)} async-done(((f32[512,1024]{1,0:T(8,128)}), f32[16,1024]{1,0:T(8,128)}) %reduce-scatter.14.cloned.1.call-update) | async-done | bytes 65552 | tf_op jit(solution)/shard_map/reduce_scatter | solution.py:86
  (59 shorter events, 13.9 us)
Async XLA Ops:
  8.0 10.6 %slice-start = ((s32[2048]{0:T(1024)}), s32[1024]{0:T(1024)S(1)}, s32[]{:S(2)}) async-start(s32[2048]{0:T(1024)} %param.13), calls=%async_computation.12 | async-start | bytes 8192 | tf_op jit(solution)/shard_map/slice | solution.py:14
  8.0 10.6 %slice-start.1 = ((s32[2048]{0:T(1024)}), s32[1024]{0:T(1024)S(1)}, s32[]{:S(2)}) async-start(s32[2048]{0:T(1024)} %param.14), calls=%async_computation.13 | async-start | bytes 8192 | tf_op jit(solution)/shard_map/slice | solution.py:14
  8.0 55.7 %all-gather.2.cloned.1.call-start = ((), (), s32[]{:S(2)}) async-start(), calls=%async_computation.7 | async-start | bytes 1081344 | tf_op jit(solution)/shard_map/all_gather | solution.py:70
  10.6 8.8 %copy-start.9 = (bf16[1024,512]{1,0:T(8,128)(2,1)S(1)}, bf16[1024,512]{1,0:T(8,128)(2,1)}, u32[]{:S(2)}) copy-start(bf16[1024,512]{1,0:T(8,128)(2,1)} %param.10) | copy-start | bytes 3145732
  10.6 24.1 %all-to-all-start = ((bf16[32,16,1024]{2,1,0:T(8,128)(2,1)}), bf16[32,16,1024]{2,1,0:T(8,128)(2,1)}, u32[]{:S(2)}, u32[]{:S(2)}) async-start(bf16[32,16,1024]{2,1,0:T(8,128)(2,1)} %stack.2), calls=%async_computation | async-start | bytes 2097152 | tf_op jit(solution)/shard_map/all_to_all | solution.py:54
  18.4 58.9 %reduce-scatter.16.cloned.1.call-start = ((), (), s32[]{:S(2)}) async-start(), calls=%async_computation.9 | async-start | bytes 1179648 | tf_op jit(solution)/shard_map/reduce_scatter | solution.py:59
  19.4 17.2 %copy-start.5 = (pred[64,8,4,256]{3,1,2,0:T(8,128)(4,1)}, pred[64,8,4,256]{3,1,2,0:T(8,128)(4,1)S(1)}, u32[]{:S(2)}) copy-start(pred[64,8,4,256]{3,1,2,0:T(8,128)(4,1)S(1)} %copy.48) | copy-start | bytes 1572868
  38.0 79.3 %reduce-scatter.18.cloned.1.call-start = ((), (), s32[]{:S(2)}) async-start(), calls=%async_computation.10 | async-start | bytes 1179648 | tf_op jit(solution)/shard_map/reduce_scatter | solution.py:60
  38.7 4.6 %copy-start = (pred[64,8,4,256]{3,1,2,0:T(8,128)(4,1)}, pred[64,8,4,256]{3,1,2,0:T(8,128)(4,1)S(1)}, u32[]{:S(2)}) copy-start(pred[64,8,4,256]{3,1,2,0:T(8,128)(4,1)S(1)} %copy.49) | copy-start | bytes 1572868
  43.3 2.7 slice-start.2
  45.9 112.0 %reduce-scatter.20.cloned.1.call-start = ((), (), s32[]{:S(2)}) async-start(), calls=%async_computation.11 | async-start | bytes 1179648 | tf_op jit(solution)/shard_map/reduce_scatter | solution.py:72
  46.8 137.5 %copy-start.7 = (pred[64,8,4,256]{3,1,2,0:T(8,128)(4,1)}, pred[64,8,4,256]{3,1,2,0:T(8,128)(4,1)S(1)}, u32[]{:S(2)}) copy-start(pred[64,8,4,256]{3,1,2,0:T(8,128)(4,1)S(1)} %copy.50) | copy-start | bytes 1572868
  69.5 203.3 %reduce-scatter.12.cloned.1.call-start = ((), (), s32[]{:S(2)}) async-start(), calls=%async_computation.6 | async-start | bytes 2162688 | tf_op jit(solution)/shard_map/reduce_scatter | solution.py:67
  187.7 175.0 %reduce-scatter.14.cloned.1.call-start = ((), (), s32[]{:S(2)}) async-start(), calls=%async_computation.8 | async-start | bytes 2162688 | tf_op jit(solution)/shard_map/reduce_scatter | solution.py:86
  238.6 2.0 copy-start.3
  238.6 2.0 copy-start.1
  242.7 1.0 copy-start.6
  247.0 3.0 copy-start.2
  247.0 3.0 copy-start.4
  253.2 3.0 copy-start.8
  253.2 3.0 copy-start.10
Sparse Core Ops, SparseCore 0:
  11.4 52.2 all-gather.1
  187.8 84.9 reduce-scatter.11
  276.6 85.9 reduce-scatter.13
Sparse Core Ops, SparseCore 1:
  38.1 39.2 reduce-scatter.15
  79.8 37.4 reduce-scatter.17
  120.2 37.6 reduce-scatter.19
